TPU v7x, 256 devices: a whole 4x4x8 slice. The times are simulated.
256 devices in a mesh: section: 8 (over z), joint: 32 (over y, x, core).
Axes of the slice: x: 4, y: 4, z: 8, core: 2. Of those that a mesh axis runs over, the one named last changes fastest.
Arguments:
- encoder_rows: bfloat16 [32, 1024, 1536], P('joint', 'section'), may hold values from -6 to 6
- up_weight: bfloat16 [1536, 3072], P(None, 'section'), may hold values from -0.15625 to 0.15625
- down_weight: bfloat16 [3072, 1536], P('section'), may hold values from -0.109375 to 0.109375
- encoder_proj: bfloat16 [1536, 640], replicated, may hold values from -0.15625 to 0.15625
- embedding: bfloat16 [4096, 640], P('joint'), may hold values from -6 to 6
- conv_taps: float32 [2, 640], replicated, may hold values from -3 to 3
- decoder_proj: bfloat16 [640, 640], replicated, may hold values from -0.25 to 0.25
- output_proj: bfloat16 [640, 4096], replicated, may hold values from -0.5 to 0.5
- output_bias: float32 [4096], replicated, may hold values from -6 to 6
- frame_lengths: int32 [32], replicated, may hold values from 1 to 1024, 20480 in all
- label_lengths: int32 [32], replicated, may hold values from 1 to 3, 48 in all
- label_ids: int32 [32, 3], replicated, may hold values from 1 to 4095
- owner_index: int32 [32], replicated, may hold values from 0 to 31, each once
Outputs:
- enc_grad: bfloat16 [32, 1024, 1536], P('joint', 'section')
- up_grad: float32 [1536, 3072], P('joint', 'section')
- down_grad: float32 [3072, 1536], P('section', 'joint')
- pred_grad: float32 [32, 4, 640], P('joint', None, 'section')
Inputs may be any that keep to these rules, and one draw needn't show every extreme that they name: `owner_index`: every joint owner receives exactly one utterance. `frame_lengths`: the longest utterance uses all 1024 frames. `label_lengths`: the longest label sequence has 3 labels. `label_ids`: never the blank token 0.
All inputs are finite; a program needn't handle non-finite values.
Results may differ from a plain program's by a relative error of at most 0.013.
Values may be sent and summed in bfloat16 or wider, within the bound.
No kernel may reach another device: no remote copies, remote signals or barrier semaphores. Data moves between devices by JAX's collectives and lax.ppermute only.
A program may use at most 128 MiB of HBM per device.

v0:
```python
import jax
import jax.numpy as jnp
from jax import lax
from jax.sharding import PartitionSpec as P

NEG_BIG = -1000000000.0


def partner_2(block, axis, bit):
    count = lax.axis_size(axis)
    route = []
    for low in range(count):
        high = low | 1 << bit
        if high != low and high < count:
            route += [(low, high), (high, low)]
    return lax.ppermute(block, axis, route)


def from_behind(value, axis, steps):
    count = lax.axis_size(axis)
    initial, last = (max(0, -steps), min(count, count - steps))
    return lax.ppermute(value, axis, [(source, source + steps) for source in range(initial, last)])


def layer_norm(values):
    average = jnp.mean(values, axis=-1, keepdims=True)
    centered = values - average
    variance = jnp.mean(centered * centered, axis=-1, keepdims=True)
    inv_scale = lax.rsqrt(variance + 1e-05)
    return (centered * inv_scale, inv_scale)


def lower_paths(label_row):
    partial_sums = jnp.concatenate([jnp.zeros((1,), jnp.float32), jnp.cumsum(label_row)])
    places = partial_sums.shape[0]
    row_ids = lax.broadcasted_iota(jnp.int32, (places, places), 0)
    col_ids = lax.broadcasted_iota(jnp.int32, (places, places), 1)
    return jnp.where(col_ids <= row_ids, partial_sums[:, None] - partial_sums[None, :], NEG_BIG)


def advance(vector, blank_row, label_row, active):
    moved = blank_row + jax.nn.logsumexp(lower_paths(label_row) + vector[None, :], axis=1)
    return jnp.where(active, moved, vector)


def run_block(vector, blank_score, label_score, active):

    def run_one_frame(carried, inputs):
        blank_row, label_row, live_flag = inputs
        return (advance(carried, blank_row, label_row, live_flag), None)

    return lax.scan(run_one_frame, vector, (blank_score, label_score, active))[0]


def block_matrix(blank_score, label_score, active):
    places = blank_score.shape[1]
    row_ids = lax.broadcasted_iota(jnp.int32, (places, places), 0)
    col_ids = lax.broadcasted_iota(jnp.int32, (places, places), 1)
    identity_map = jnp.where(row_ids == col_ids, 0.0, NEG_BIG)

    def block_one_frame(carried, inputs):
        blank_row, label_row, live_flag = inputs
        moved = blank_row[:, None] + jax.nn.logsumexp(
            lower_paths(label_row)[:, :, None] + carried[None, :, :], axis=1
        )
        return (jnp.where(live_flag, moved, carried), None)

    return lax.scan(block_one_frame, identity_map, (blank_score, label_score, active))[0]


def log_apply(transfer, vector):
    return jax.nn.logsumexp(transfer + vector[None, :], axis=1)


def log_apply_back(transfer, vector):
    return jax.nn.logsumexp(transfer + vector[:, None], axis=0)


def joint_forward(frame_part, pred_here, label_row_ids, output_proj, output_bias):
    joined = jnp.tanh(frame_part.astype(jnp.float32)[:, None, :] + pred_here[None, :, :]).astype(
        jnp.bfloat16
    )
    frames_here, places, joint_width = joined.shape
    logits = (
        jnp.dot(
            joined.reshape(frames_here * places, joint_width),
            output_proj,
            preferred_element_type=jnp.float32,
        )
        + output_bias
    )
    logits = logits.reshape(frames_here, places, -1)
    exponent = jnp.exp(logits)
    denominator = jnp.sum(exponent, axis=-1, keepdims=True)
    log_total = jnp.log(denominator)[:, :, 0]
    blank_score = logits[:, :, 0] - log_total
    index_grid = jnp.broadcast_to(label_row_ids[None, :, None], (frames_here, places - 1, 1))
    picked = jnp.take_along_axis(logits[:, :-1, :], index_grid, axis=2)[:, :, 0]
    label_score = picked - log_total[:, :-1]
    posterior = exponent / denominator
    return (joined, posterior, blank_score, label_score)


def joint_backward(blank_grad, label_grad, label_row_ids, joined, posterior, output_proj):
    frames_here, places, vocab_size = posterior.shape
    label_full = jnp.pad(label_grad, ((0, 0), (0, 1)))
    weight_sum = blank_grad + label_full
    token_full = jnp.concatenate([label_row_ids, jnp.full((1,), -1, jnp.int32)])
    vocab_iota = lax.broadcasted_iota(jnp.int32, (1, 1, vocab_size), 2)
    blank_term = jnp.where(vocab_iota == 0, blank_grad[:, :, None], 0.0)
    label_term = jnp.where(vocab_iota == token_full[None, :, None], label_full[:, :, None], 0.0)
    logit_grad = -posterior * weight_sum[:, :, None] + blank_term + label_term
    logit_grad = logit_grad.astype(jnp.bfloat16).reshape(frames_here * places, vocab_size)
    joined_grad = lax.dot_general(
        logit_grad, output_proj, (((1,), (1,)), ((), ())), preferred_element_type=jnp.float32
    )
    joined_vals = joined.astype(jnp.float32).reshape(frames_here * places, -1)
    inner_grad = (joined_grad * (1.0 - joined_vals * joined_vals)).reshape(frames_here, places, -1)
    frame_part_grad = jnp.sum(inner_grad, axis=1).astype(jnp.bfloat16)
    pred_part_grad = jnp.sum(inner_grad, axis=0)
    return (frame_part_grad, pred_part_grad)


def network_sections(count):
    sections = []
    block_size = 2
    while block_size <= count:
        stride = block_size // 2
        while stride >= 1:
            sections.append((block_size, stride))
            stride = stride // 2
        block_size = block_size * 2
    return sections


def sort_section(keys, block_size, stride, device_id):
    count = keys.shape[0]
    position = jnp.arange(count, dtype=jnp.int32)
    partner = position ^ stride
    partner_keys = keys[partner]
    rising = position & block_size == 0
    lower_side = position < partner
    keep_small = lower_side == rising
    new_keys = jnp.where(
        keep_small, jnp.minimum(keys, partner_keys), jnp.maximum(keys, partner_keys)
    )
    takes = new_keys[device_id] != keys[device_id]
    return (new_keys, takes)


def route_owner(payload, keys, device_id, count):
    for block_size, stride in network_sections(count):
        keys, takes = sort_section(keys, block_size, stride, device_id)
        other = partner_2(payload, "joint", stride.bit_length() - 1)
        payload = jnp.where(takes, other, payload)
    return payload


def route_holder(payload, keys, device_id, count):
    for block_size, stride in network_sections(count):
        keys, takes = sort_section(keys, block_size, stride, device_id)
        other = partner_2(payload, "joint", stride.bit_length() - 1)
        payload = jnp.where(takes, other, payload)
    return payload


def on_device(
    encoder_rows,
    up_weight,
    down_weight,
    encoder_proj,
    embedding,
    conv_taps,
    decoder_proj,
    output_proj,
    output_bias,
    frame_lengths,
    label_lengths,
    label_ids,
    owner_index,
):
    section_count = lax.axis_size("section")
    joint_count = lax.axis_size("joint")
    section_id = lax.axis_index("section")
    joint_id = lax.axis_index("joint")
    block_len = encoder_rows.shape[1]
    utterances = label_ids.shape[0]
    places = label_ids.shape[1] + 1
    own_rows = encoder_rows[0].astype(jnp.float32)
    normed_in = layer_norm(own_rows)[0].astype(jnp.bfloat16)
    gathered = lax.all_gather(normed_in, "section", axis=0, tiled=True)
    pre_hidden = jnp.dot(gathered, up_weight, preferred_element_type=jnp.float32)
    hidden = jax.nn.silu(pre_hidden).astype(jnp.bfloat16)
    encoded = own_rows + lax.psum_scatter(
        0.5 * jnp.dot(hidden, down_weight, preferred_element_type=jnp.float32),
        "section",
        scatter_dimension=0,
        tiled=True,
    )
    unit_rows, inv_scale = layer_norm(encoded)
    frame_part = jnp.dot(
        unit_rows.astype(jnp.bfloat16), encoder_proj, preferred_element_type=jnp.float32
    ).astype(jnp.bfloat16)
    order_iota = jnp.arange(utterances, dtype=jnp.int32)
    inverse = jnp.zeros((utterances,), jnp.int32).at[owner_index].set(order_iota)
    own_utterance = inverse[joint_id]
    owner_frames = route_owner(frame_part, owner_index, joint_id, joint_count)
    context = jnp.concatenate([jnp.zeros((utterances, 1), jnp.int32), label_ids], axis=1)
    vocab_rows = embedding.shape[0]
    vocab_ids = joint_id * vocab_rows + jnp.arange(vocab_rows, dtype=jnp.int32)

    def label_term(start_row, row_count):
        number = row_count // places
        wanted = context[inverse].reshape(number * places)
        selector = (wanted[:, None] == vocab_ids[None, :]).astype(jnp.bfloat16)
        return jnp.dot(selector, embedding, preferred_element_type=jnp.float32)

    looked = lax.psum_scatter(
        label_term(jnp.int32(0), places * lax.axis_size("joint")).astype(jnp.bfloat16),
        "joint",
        scatter_dimension=0,
        tiled=True,
    ).astype(jnp.float32)
    previous = jnp.concatenate([looked[:1], looked[:-1]], axis=0)
    pred_act = jnp.maximum(conv_taps[0] * previous + conv_taps[1] * looked, 0.0).astype(
        jnp.bfloat16
    )
    pred_rows = jnp.dot(pred_act, decoder_proj, preferred_element_type=jnp.float32)
    label_here = label_ids[own_utterance]
    frames_used = frame_lengths[own_utterance]
    labels_used = label_lengths[own_utterance]
    joined, posterior, blank_score, label_score = joint_forward(
        owner_frames, pred_rows, label_here, output_proj, output_bias
    )
    frame_ids = section_id * block_len + jnp.arange(block_len, dtype=jnp.int32)
    active = frame_ids < frames_used
    transfer = block_matrix(blank_score, label_score, active)
    place_iota = jnp.arange(places, dtype=jnp.int32)
    start_vec = jnp.where(place_iota == 0, 0.0, NEG_BIG)
    finish_vec = jnp.where(place_iota == labels_used, 0.0, NEG_BIG)

    def forward_turn(turn_index, carried):
        passed = from_behind(log_apply(transfer, carried), "section", 1)
        return jnp.where(section_id == 0, start_vec, passed)

    incoming = lax.fori_loop(0, section_count - 1, forward_turn, start_vec)

    def backward_turn(turn_index, carried):
        passed = from_behind(log_apply_back(transfer, carried), "section", -1)
        return jnp.where(section_id == section_count - 1, finish_vec, passed)

    leaving = lax.fori_loop(0, section_count - 1, backward_turn, finish_vec)

    def block_out(blank_in, label_in):
        return run_block(incoming, blank_in, label_in, active)

    end_alpha, pullback = jax.vjp(block_out, blank_score, label_score)
    logprob = jax.nn.logsumexp(end_alpha + leaving)
    blank_grad, label_grad = pullback(-jnp.exp(end_alpha + leaving - logprob))
    frame_part_grad, pred_part = joint_backward(
        blank_grad, label_grad, label_here, joined, posterior, output_proj
    )
    part_grad = route_holder(frame_part_grad, inverse, joint_id, joint_count)
    unit_grad = lax.dot_general(
        part_grad, encoder_proj, (((1,), (1,)), ((), ())), preferred_element_type=jnp.float32
    )
    first_mean = jnp.mean(unit_grad, axis=-1, keepdims=True)
    second_mean = jnp.mean(unit_grad * unit_rows, axis=-1, keepdims=True)
    row_grad = (inv_scale * (unit_grad - first_mean - unit_rows * second_mean)).astype(jnp.bfloat16)
    grad_all = lax.all_gather(row_grad, "section", axis=0, tiled=True)
    hidden_grad = 0.5 * lax.dot_general(
        grad_all, down_weight, (((1,), (1,)), ((), ())), preferred_element_type=jnp.float32
    )
    gate_sigmoid = jax.nn.sigmoid(pre_hidden)
    pre_grad = (hidden_grad * gate_sigmoid * (1.0 + pre_hidden * (1.0 - gate_sigmoid))).astype(
        jnp.bfloat16
    )
    up_part = lax.dot_general(
        gathered, pre_grad, (((0,), (0,)), ((), ())), preferred_element_type=jnp.float32
    )
    down_part = 0.5 * lax.dot_general(
        hidden, grad_all, (((0,), (0,)), ((), ())), preferred_element_type=jnp.float32
    )
    up_sum, down_sum = (
        lax.psum_scatter(
            up_part.astype(jnp.bfloat16), "joint", scatter_dimension=0, tiled=True
        ).astype(jnp.float32),
        lax.psum_scatter(
            down_part.astype(jnp.bfloat16), "joint", scatter_dimension=1, tiled=True
        ).astype(jnp.float32),
    )
    pred_sum = lax.psum_scatter(pred_part[None], "section", scatter_dimension=2, tiled=True)
    return (row_grad[None], up_sum, down_sum, pred_sum)


def solution(mesh):
    return jax.shard_map(
        on_device,
        mesh=mesh,
        in_specs=(
            P("joint", "section", None),
            P(None, "section"),
            P("section", None),
            P(),
            P("joint", None),
            P(),
            P(),
            P(),
            P(),
            P(),
            P(),
            P(),
            P(),
        ),
        out_specs=(
            P("joint", "section", None),
            P("joint", "section"),
            P("section", "joint"),
            P("joint", None, "section"),
        ),
        check_vma=False,
    )
```

profile of v0, /device:TPU:2, one launch (start us, length us, event | category | flops | bytes accessed | tf_op | source)
XLA Modules:
  0.0 2108.3 jit_solution(6235568972007815648)
XLA Ops:
  12.7 48.0 %all-gather.3.cloned.1.call-done = bf16[1024,1536]{1,0:T(8,128)(2,1)} async-done(((bf16[128,1536]{1,0:T(8,128)(2,1)}), bf16[1024,1536]{1,0:T(8,128)(2,1)}) %all-gather.3.cloned.1.call-update) | async-done | bytes 3145744 | tf_op jit(solution)/shard_map/all_gather | solution.py:191
  65.7 4.5 convolution_multiply_fusion
  86.9 57.3 %reduce-scatter.7.cloned.1.call-done = f32[128,1536]{1,0:T(8,128)} async-done(((f32[1024,1536]{1,0:T(8,128)}), f32[128,1536]{1,0:T(8,128)}) %reduce-scatter.7.cloned.1.call-update) | async-done | bytes 786448 | tf_op jit(solution)/shard_map/reduce_scatter | solution.py:194
  179.8 5.0 collective-permute-done.8
  232.5 6.8 broadcast_in_dim.223
  246.4 9.4 exponential_reduce_fusion.3
  255.9 9.8 reshape.609
  266.7 5.5 gather_fusion.31
  275.0 308.2 %while.74 = (s32[]{:T(128)}, f32[4,4]{1,0:T(4,128)S(1)}, pred[128]{0:T(512)(128)(4,1)S(1)}, f32[128,4]{1,0:T(8,128)S(1)}, f32[128,3]{1,0:T(8,128)}, /*index=5*/s32[]{:T(128)}, f32[]{:T(128)}, f32[1]{0:T(128)}) while((s32[]{:T(128)}, f32[4,4]{1,0:T(4,128)S(1)}, pred[128]{0:T(512)(128)(4,1)S(1)}, f32[128,4]{1,0:T(8,128)S(1)}, ...), condition=%wide.region_12.13_spmd, body=%wide.region_8.0_spmd.sunk | while | flops 476 | bytes 1144 | solution.py:68
  583.2 39.8 %while.75 = (s32[]{:T(128)}, f32[4]{0:T(128)S(1)}, pred[]{:T(512)}, f32[4,4]{1,0:T(4,128)S(1)}, s32[]{:T(128)}) while((s32[]{:T(128)}, f32[4]{0:T(128)S(1)}, pred[]{:T(512)}, f32[4,4]{1,0:T(4,128)S(1)}, s32[]{:T(128)}) %tuple.157), condition=%wide.region_16.17_spmd.clone, body=%wide.region_13.16_spmd.clone.sunk | while | flops 110 | bytes 486 | solution.py:246
  610.0 4.7 collective-permute-start
  616.3 5.4 collective-permute-start
  623.0 567.5 %while.78 = (s32[]{:T(128)}, f32[4]{0:T(128)S(1)}, f32[128,4,4]{2,1,0:T(4,128)}, pred[128,4]{1,0:T(8,128)(4,1)}, f32[128,4]{1,0:T(8,128)S(1)}, /*index=5*/pred[1...) while((s32[]{:T(128)}, f32[4]{0:T(128)S(1)}, ...), condition=%wide.region_21.22_spmd.clone.clone, body=%wide.region_17.21_spmd.clone.clone.sunk | while | flops 296 | bytes 5132 | solution.py:52
  1190.5 53.7 %while.76 = (s32[]{:T(128)}, f32[4]{0:T(128)S(1)}, pred[]{:T(512)}, f32[4,4]{1,0:T(4,128)S(1)}, s32[]{:T(128)}, /*index=5*/s32[]{:T(128)}) while((s32[]{:T(128)}, f32[4]{0:T(128)S(1)}, pred[]{:T(512)}, f32[4,4]{1,0:T(4,128)S(1)}, s32[]{:T(128)}, /*index=5*/s32[]{:T(128)}) %tuple.183), condition=%wide.region_25.26_spmd.clone, body=%wide.region_22.25_spmd.clone.sunk | while | flops 110 | bytes 498 | solution.py:252
  1192.0 5.6 collective-permute-done.1
  1199.7 5.6 collective-permute-done.1
  1207.5 5.6 collective-permute-done.1
  1215.3 5.6 collective-permute-done.1
  1223.1 5.4 collective-permute-done.1
  1230.6 5.4 collective-permute-done.1
  1238.1 5.4 collective-permute-done.1
  1247.4 484.2 %while.77 = (s32[]{:T(128)}, f32[4]{0:T(128)S(1)}, f32[128,4]{1,0:T(8,128)S(1)}, f32[128,3]{1,0:T(8,128)S(1)}, pred[128]{0:T(512)(128)(4,1)S(1)}, /*index=5*/pre...) while((s32[]{:T(128)}, f32[4]{0:T(128)S(1)}, ...), condition=%wide.region_33.34_spmd.clone, body=%wide.region_28.33_spmd.clone.sunk | while | flops 133 | bytes 553 | solution.py:52
  1731.9 12.4 fusion.31
  1766.4 4.6 collective-permute-done.20
  1788.3 5.2 collective-permute-start.24
  1822.1 5.0 collective-permute-start.29
  1843.2 49.4 %all-gather.5.cloned.1.call-done = bf16[1024,1536]{1,0:T(8,128)(2,1)} async-done(((bf16[128,1536]{1,0:T(8,128)(2,1)}), bf16[1024,1536]{1,0:T(8,128)(2,1)}) %all-gather.5.cloned.1.call-update) | async-done | bytes 3145744 | tf_op jit(solution)/shard_map/all_gather | solution.py:270
  1892.6 5.3 fusion.30
  1898.0 7.8 convolution_convert_fusion
  1905.8 25.1 %reduce-scatter.13.cloned.1.call-done = f32[80,4]{1,0:T(8,128)} async-done(((f32[640,4]{1,0:T(8,128)}), f32[80,4]{1,0:T(8,128)}) %reduce-scatter.13.cloned.1.call-update) | async-done | bytes 1296
  1932.3 82.1 %reduce-scatter.11.cloned.1.call-done = bf16[384,48]{0,1:T(8,128)(2,1)} async-done(((bf16[384,1536]{0,1:T(8,128)(2,1)}), bf16[384,48]{0,1:T(8,128)(2,1)}) %reduce-scatter.11.cloned.1.call-update) | async-done | bytes 36880 | tf_op jit(solution)/shard_map/reduce_scatter | solution.py:288
  2015.8 83.2 %reduce-scatter.9.cloned.1.call-done = bf16[48,384]{1,0:T(8,128)(2,1)} async-done(((bf16[1536,384]{1,0:T(8,128)(2,1)}), bf16[48,384]{1,0:T(8,128)(2,1)}) %reduce-scatter.9.cloned.1.call-update) | async-done | bytes 36880 | tf_op jit(solution)/shard_map/reduce_scatter | solution.py:285
  (4265 shorter events, 1567.4 us)
Async XLA Ops:
  8.0 52.7 %all-gather.3.cloned.1.call-start = ((), (), s32[]{:S(2)}) async-start(), calls=%async_computation.4 | async-start | bytes 3538944 | tf_op jit(solution)/shard_map/all_gather | solution.py:191
  12.6 131.5 %reduce-scatter.7.cloned.1.call-start = ((), (), s32[]{:S(2)}) async-start(), calls=%async_computation.5 | async-start | bytes 7077888 | tf_op jit(solution)/shard_map/reduce_scatter | solution.py:194
  70.2 170.3 %all-reduce.5.cloned.1.call-start = ((), (), s32[]{:S(2)}) async-start(), calls=%async_computation.10 | async-start | bytes 327680
  74.8 1817.9 %all-gather.5.cloned.1.call-start = ((), (), s32[]{:S(2)}) async-start(), calls=%async_computation.6 | async-start | bytes 3538944 | tf_op jit(solution)/shard_map/all_gather | solution.py:270
  149.0 7.0 collective-permute-start.3
  160.2 7.8 collective-permute-start.5
  168.0 8.9 collective-permute-start.6
  178.4 6.4 collective-permute-start.8
  184.8 7.0 collective-permute-start.9
  191.9 6.3 collective-permute-start.10
  200.3 7.8 collective-permute-start.12
  213.7 6.9 collective-permute-start.14
  222.2 19.1 collective-permute-start.15
  610.0 6.0 collective-permute-start
  616.3 6.7 collective-permute-start
  1190.7 6.9 collective-permute-start.1
  1198.4 6.9 collective-permute-start.1
  1206.2 6.9 collective-permute-start.1
  1214.0 6.9 collective-permute-start.1
  1221.8 6.7 collective-permute-start.1
  1229.3 6.7 collective-permute-start.1
  1236.8 6.7 collective-permute-start.1
  1752.1 6.8 collective-permute-start.18
  1763.1 7.8 collective-permute-start.20
  1780.2 8.0 collective-permute-start.23
  1788.3 9.5 collective-permute-start.24
  1797.8 6.5 collective-permute-start.25
  1808.3 8.0 collective-permute-start.27
  1822.1 8.6 collective-permute-start.29
  1842.2 88.7 %reduce-scatter.13.cloned.1.call-start = ((), (), s32[]{:S(2)}) async-start(), calls=%async_computation.9 | async-start | bytes 368640
  1843.2 171.3 %reduce-scatter.11.cloned.1.call-start = ((), (), s32[]{:S(2)}) async-start(), calls=%async_computation.8 | async-start | bytes 1216512 | tf_op jit(solution)/shard_map/reduce_scatter | solution.py:288
  1897.9 201.1 %reduce-scatter.9.cloned.1.call-start = ((), (), s32[]{:S(2)}) async-start(), calls=%async_computation.7 | async-start | bytes 1216512 | tf_op jit(solution)/shard_map/reduce_scatter | solution.py:285
  (47 other events, 2084.4 us)
Sparse Core Ops, SparseCore 0:
  12.8 47.9 all-gather.2
  70.3 73.7 reduce-scatter.6
  1842.3 50.2 all-gather.4
  1895.0 35.8 reduce-scatter.12
  1934.6 79.7 reduce-scatter.10
  2018.1 80.8 reduce-scatter.8
Sparse Core Ops, SparseCore 1:
  74.9 107.8 all-reduce.4
where the time goes:
time: 2140 us; the launch traced here: 2110 us
  other arithmetic  813 us (38%)
  local copies, waits for them, and re-layouts  667 us (31%)
  waiting for transfers between devices  437 us (20%)
  starting transfers between devices  79.3 us (4%)
  between operations  60.3 us (3%)
  matrix products  46.8 us (2%)
    dynamic_slice x384, local copies, waits for them, and re-layouts, block_matrix(): lax.scan(block_one_frame, identity_map, (blank_score, label_score, active))  219 us
    another operation x386, local copies, waits for them, and re-layouts  187 us
    dynamic_update_slice x512, local copies, waits for them, and re-layouts, run_block(): lax.scan(run_one_frame, vector, (blank_score, label_score, active))[0]  173 us
    broadcast_in_dim x130, other arithmetic, run_block(): lax.scan(run_one_frame, vector, (blank_score, label_score, active))[0]  171 us
    reduce_sum x128, other arithmetic, lower_paths(): partial_sums[:, None] - partial_sums[None, :]  112 us
    dynamic_update_slice x128, other arithmetic, run_block(): lax.scan(run_one_frame, vector, (blank_score, label_score, active))[0]  84.6 us
    add_any x128, other arithmetic, advance(): vector[None, :]  84.1 us
    reduce_scatter x1, waiting for transfers between devices, on_device(): lax.psum_scatter(up_part.astype(jnp.bfloat16), 'joint', scatter_dimension...  83.2 us

commit v1 on v0

--- a/solution.py
+++ b/solution.py
@@ -4,6 +4,16 @@
 from jax.sharding import PartitionSpec as P
 
 NEG_BIG = -1000000000.0
+
+
+def wait_body_in(frame, dev_axis):
+    ready = jnp.concatenate(
+        jax.lax.all_to_all(
+            jnp.stack([frame] * jax.lax.axis_size(dev_axis), axis=0), dev_axis, 0, 0
+        ),
+        0,
+    )
+    return ready
 
 
 def partner_2(block, axis, bit):
@@ -267,7 +277,7 @@
     first_mean = jnp.mean(unit_grad, axis=-1, keepdims=True)
     second_mean = jnp.mean(unit_grad * unit_rows, axis=-1, keepdims=True)
     row_grad = (inv_scale * (unit_grad - first_mean - unit_rows * second_mean)).astype(jnp.bfloat16)
-    grad_all = lax.all_gather(row_grad, "section", axis=0, tiled=True)
+    grad_all = wait_body_in(row_grad, dev_axis="section")
     hidden_grad = 0.5 * lax.dot_general(
         grad_all, down_weight, (((1,), (1,)), ((), ())), preferred_element_type=jnp.float32
     )

time: 2140 us -> 2190 us (1.023)
  other arithmetic: 813 us -> 836 us
    all_to_all x0 -> x1, waiting for transfers between devices: none -> 76.5 us  [wait_body_in(): jax.lax.all_to_all(jnp.stack([frame] * jax.lax.axis_size(dev_axis), axis=...]
    all_gather x1 -> x0, waiting for transfers between devices: 49.4 us -> none  [on_device(): grad_all = lax.all_gather(row_grad, 'section', axis=0, tiled=True)]
    unnamed x9 -> x8, waiting for transfers between devices: 25.2 us -> 0.15 us
    another operation x386 -> x387, local copies, waits for them, and re-layouts: 187 us -> 189 us
where the time goes in v1:
time: 2190 us; the launch traced here: 2150 us
  other arithmetic  836 us (38%)
  local copies, waits for them, and re-layouts  686 us (31%)
  waiting for transfers between devices  427 us (19%)
  starting transfers between devices  90.1 us (4%)
  between operations  59.8 us (3%)
  matrix products  46.8 us (2%)
    dynamic_slice x384, local copies, waits for them, and re-layouts, block_matrix(): lax.scan(block_one_frame, identity_map, (blank_score, label_score, active))  237 us
    another operation x386, local copies, waits for them, and re-layouts  187 us
    dynamic_update_slice x512, local copies, waits for them, and re-layouts, run_block(): lax.scan(run_one_frame, vector, (blank_score, label_score, active))[0]  173 us
    broadcast_in_dim x130, other arithmetic, run_block(): lax.scan(run_one_frame, vector, (blank_score, label_score, active))[0]  171 us
    reduce_sum x128, other arithmetic, lower_paths(): partial_sums[:, None] - partial_sums[None, :]  112 us
    select_n x128, other arithmetic, block_one_frame(): return (jnp.where(live_flag, moved, carried), None)  96.1 us
    dynamic_update_slice x128, other arithmetic, run_block(): lax.scan(run_one_frame, vector, (blank_score, label_score, active))[0]  84.6 us
    add_any x128, other arithmetic, advance(): vector[None, :]  84.1 us

profile of v1, /device:TPU:2, one launch (start us, length us, event | category | flops | bytes accessed | tf_op | source)
XLA Modules:
  0.0 2151.8 jit_solution(12089889038722543542)
XLA Ops:
  12.7 48.0 %all-gather.2.cloned.1.call-done = bf16[1024,1536]{1,0:T(8,128)(2,1)} async-done(((bf16[128,1536]{1,0:T(8,128)(2,1)}), bf16[1024,1536]{1,0:T(8,128)(2,1)}) %all-gather.2.cloned.1.call-update) | async-done | bytes 3145744 | tf_op jit(solution)/shard_map/all_gather | solution.py:201
  65.7 4.5 convolution_multiply_fusion
  86.8 57.3 %reduce-scatter.7.cloned.1.call-done = f32[128,1536]{1,0:T(8,128)} async-done(((f32[1024,1536]{1,0:T(8,128)}), f32[128,1536]{1,0:T(8,128)}) %reduce-scatter.7.cloned.1.call-update) | async-done | bytes 786448 | tf_op jit(solution)/shard_map/reduce_scatter | solution.py:204
  178.9 5.6 collective-permute-done.8
  231.5 6.8 broadcast_in_dim.223
  245.4 9.4 exponential_reduce_fusion.3
  254.8 9.8 reshape.614
  265.6 5.5 gather_fusion.31
  273.9 337.9 %while.74 = (s32[]{:T(128)}, f32[4,4]{1,0:T(4,128)S(1)}, pred[128]{0:T(512)(128)(4,1)S(1)}, f32[128,4]{1,0:T(8,128)S(1)}, f32[128,3]{1,0:T(8,128)}, /*index=5*/s32[]{:T(128)}, f32[]{:T(128)}, f32[1]{0:T(128)}) while((s32[]{:T(128)}, f32[4,4]{1,0:T(4,128)S(1)}, pred[128]{0:T(512)(128)(4,1)S(1)}, f32[128,4]{1,0:T(8,128)S(1)}, ...), condition=%wide.region_12.13_spmd, body=%wide.region_8.0_spmd.sunk | while | flops 476 | bytes 1144 | solution.py:78
  611.7 39.8 %while.75 = (s32[]{:T(128)}, f32[4]{0:T(128)S(1)}, pred[]{:T(512)}, f32[4,4]{1,0:T(4,128)S(1)}, s32[]{:T(128)}) while((s32[]{:T(128)}, f32[4]{0:T(128)S(1)}, pred[]{:T(512)}, f32[4,4]{1,0:T(4,128)S(1)}, s32[]{:T(128)}) %tuple.157), condition=%wide.region_16.17_spmd.clone, body=%wide.region_13.16_spmd.clone.sunk | while | flops 110 | bytes 486 | solution.py:256
  638.5 4.8 collective-permute-start
  644.9 5.4 collective-permute-start
  651.6 582.1 %while.78 = (s32[]{:T(128)}, f32[4]{0:T(128)S(1)}, f32[128,4,4]{2,1,0:T(4,128)}, pred[128,4]{1,0:T(8,128)(4,1)}, f32[128,4]{1,0:T(8,128)S(1)}, /*index=5*/pred[1...) while((s32[]{:T(128)}, f32[4]{0:T(128)S(1)}, ...), condition=%wide.region_21.22_spmd.clone.clone, body=%wide.region_17.21_spmd.clone.clone.sunk | while | flops 296 | bytes 5132 | solution.py:62
  1233.7 53.7 %while.76 = (s32[]{:T(128)}, f32[4]{0:T(128)S(1)}, pred[]{:T(512)}, f32[4,4]{1,0:T(4,128)S(1)}, s32[]{:T(128)}, /*index=5*/s32[]{:T(128)}) while((s32[]{:T(128)}, f32[4]{0:T(128)S(1)}, pred[]{:T(512)}, f32[4,4]{1,0:T(4,128)S(1)}, s32[]{:T(128)}, /*index=5*/s32[]{:T(128)}) %tuple.181), condition=%wide.region_25.26_spmd.clone, body=%wide.region_22.25_spmd.clone.sunk | while | flops 110 | bytes 498 | solution.py:262
  1235.1 5.6 collective-permute-done.1
  1242.9 5.6 collective-permute-done.1
  1250.7 5.6 collective-permute-done.1
  1258.5 5.6 collective-permute-done.1
  1266.3 5.4 collective-permute-done.1
  1273.8 5.4 collective-permute-done.1
  1281.3 5.4 collective-permute-done.1
  1290.6 484.2 %while.77 = (s32[]{:T(128)}, f32[4]{0:T(128)S(1)}, f32[128,4]{1,0:T(8,128)S(1)}, f32[128,3]{1,0:T(8,128)S(1)}, pred[128]{0:T(512)(128)(4,1)S(1)}, /*index=5*/pre...) while((s32[]{:T(128)}, f32[4]{0:T(128)S(1)}, ...), condition=%wide.region_33.34_spmd.clone, body=%wide.region_28.33_spmd.clone.sunk | while | flops 133 | bytes 553 | solution.py:62
  1775.1 12.3 fusion.31
  1809.8 4.3 collective-permute-done.20
  1831.7 5.2 collective-permute-start.24
  1865.6 5.0 collective-permute-start.29
  1887.0 9.8 all-to-all-start
  1897.9 76.5 %all-to-all-done = bf16[8,128,1536]{2,1,0:T(8,128)(2,1)} async-done(((bf16[8,128,1536]{2,1,0:T(8,128)(2,1)}), bf16[8,128,1536]{2,1,0:T(8,128)(2,1)}, u32[]{:S(2)}, u32[]{:S(2)}) %all-to-all-start) | async-done | bytes 3145760 | tf_op jit(solution)/shard_map/all_to_all | solution.py:11
  1974.4 5.4 fusion.30
  1979.8 7.8 convolution_convert_fusion
  1989.1 69.2 %reduce-scatter.11.cloned.1.call-done = bf16[384,48]{0,1:T(8,128)(2,1)} async-done(((bf16[384,1536]{0,1:T(8,128)(2,1)}), bf16[384,48]{0,1:T(8,128)(2,1)}) %reduce-scatter.11.cloned.1.call-update) | async-done | bytes 36880 | tf_op jit(solution)/shard_map/reduce_scatter | solution.py:298
  2059.7 83.1 %reduce-scatter.9.cloned.1.call-done = bf16[48,384]{1,0:T(8,128)(2,1)} async-done(((bf16[1536,384]{1,0:T(8,128)(2,1)}), bf16[48,384]{1,0:T(8,128)(2,1)}) %reduce-scatter.9.cloned.1.call-update) | async-done | bytes 36880 | tf_op jit(solution)/shard_map/reduce_scatter | solution.py:295
  (4275 shorter events, 1612.2 us)
Async XLA Ops:
  8.0 52.7 %all-gather.2.cloned.1.call-start = ((), (), s32[]{:S(2)}) async-start(), calls=%async_computation.5 | async-start | bytes 3538944 | tf_op jit(solution)/shard_map/all_gather | solution.py:201
  12.7 131.5 %reduce-scatter.7.cloned.1.call-start = ((), (), s32[]{:S(2)}) async-start(), calls=%async_computation.6 | async-start | bytes 7077888 | tf_op jit(solution)/shard_map/reduce_scatter | solution.py:204
  70.2 169.3 %all-reduce.5.cloned.1.call-start = ((), (), s32[]{:S(2)}) async-start(), calls=%async_computation.10 | async-start | bytes 327680
  149.0 6.9 collective-permute-start.3
  160.2 7.8 collective-permute-start.5
  168.0 8.5 collective-permute-start.6
  178.1 6.4 collective-permute-start.8
  184.5 7.0 collective-permute-start.9
  191.6 6.3 collective-permute-start.10
  199.9 7.8 collective-permute-start.12
  213.3 6.9 collective-permute-start.14
  221.8 18.4 collective-permute-start.15
  638.5 6.1 collective-permute-start
  644.9 6.7 collective-permute-start
  1233.8 6.9 collective-permute-start.1
  1241.6 6.9 collective-permute-start.1
  1249.4 6.9 collective-permute-start.1
  1257.2 6.9 collective-permute-start.1
  1265.0 6.7 collective-permute-start.1
  1272.5 6.7 collective-permute-start.1
  1280.0 6.7 collective-permute-start.1
  1795.3 6.8 collective-permute-start.18
  1806.3 7.8 collective-permute-start.20
  1823.5 8.2 collective-permute-start.23
  1831.7 9.5 collective-permute-start.24
  1841.3 6.5 collective-permute-start.25
  1851.9 8.0 collective-permute-start.27
  1865.6 8.6 collective-permute-start.29
  1887.0 87.3 %all-to-all-start = ((bf16[8,128,1536]{2,1,0:T(8,128)(2,1)}), bf16[8,128,1536]{2,1,0:T(8,128)(2,1)}, u32[]{:S(2)}, u32[]{:S(2)}) async-start(bf16[8,128,1536]{2,1,0:T(8,128)(2,1)} %stack.2), calls=%async_computation.1 | async-start | bytes 6291456 | tf_op jit(solution)/shard_map/all_to_all | solution.py:11
  1896.8 90.8 %reduce-scatter.13.cloned.1.call-start = ((), (), s32[]{:S(2)}) async-start(), calls=%async_computation.9 | async-start | bytes 368640
  1897.8 160.5 %reduce-scatter.11.cloned.1.call-start = ((), (), s32[]{:S(2)}) async-start(), calls=%async_computation.8 | async-start | bytes 1216512 | tf_op jit(solution)/shard_map/reduce_scatter | solution.py:298
  1979.8 163.1 %reduce-scatter.9.cloned.1.call-start = ((), (), s32[]{:S(2)}) async-start(), calls=%async_computation.7 | async-start | bytes 1216512 | tf_op jit(solution)/shard_map/reduce_scatter | solution.py:295
  (52 other events, 2181.1 us)
Sparse Core Ops, SparseCore 0:
  12.8 47.9 all-gather.1
  70.4 73.7 reduce-scatter.6
  1900.2 46.8 reduce-scatter.12
  1979.9 78.4 reduce-scatter.10
  2062.0 80.7 reduce-scatter.8
Sparse Core Ops, SparseCore 1:
  74.9 107.9 all-reduce.4
